TPU v7x, 256 devices: a whole 4x4x8 slice. The times are simulated.
256 devices in a mesh: space: 64 (over x, z, core), tm: 4 (over y).
Axes of the slice: x: 4, y: 4, z: 8, core: 2. Of those that a mesh axis runs over, the one named last changes fastest.
Arguments:
- snapshots: float32 [4608, 65536], P('tm', 'space'), as said below
- block_starts: int32 [32], P('tm'), may hold values from 0 to 4352, as said below
- owner: int32 [9], replicated, may hold values from 0 to 3, as said below
Outputs:
- modes: float32 [20, 32, 2, 65536], P('tm', None, None, 'space')
Inputs may be any that keep to these rules, and one draw needn't show every extreme that they name: `block_starts`: block k lies inside the snapshots held by index k // 8 of tm: its start is that range's first snapshot plus an even offset of 0 to 896; within one range the starts rise with k by 112 or more, the range's first block starts at offset 0 and its last at 896. `owner`: one index of tm owns exactly 5 frequencies, every other index owns one or more and fewer than 5. `snapshots`: finite real values.
All inputs are finite; a program needn't handle non-finite values.
Results may differ from a plain program's by a relative error of at most 0.0003.
Values sent between devices are 32-bit elements; how exact they have to be, the bound alone decides.
No kernel may reach another device: no remote copies, remote signals or barrier semaphores. Data moves between devices by JAX's collectives and lax.ppermute only.
A program may use at most 64 MiB of HBM per device.

v0:
```python
import jax
import jax.numpy as jnp
from jax import lax
from jax.sharding import PartitionSpec as P

NFFT = 256
NF = 9
FCAP = 5


def dft_table():
    times = jnp.arange(NFFT, dtype=jnp.int32)
    freqs = jnp.arange(NF, dtype=jnp.int32)
    phase = freqs[:, None] * times[None, :] % NFFT
    angle = 2.0 * jnp.pi / NFFT * phase.astype(jnp.float32)
    window = 0.5 - 0.5 * jnp.cos(2.0 * jnp.pi / NFFT * times.astype(jnp.float32))
    return jnp.stack([window * jnp.cos(angle), -window * jnp.sin(angle)], axis=1)


def slot_selector(owner, slot_count):
    freq_ids = jnp.arange(owner.shape[0], dtype=jnp.int32)
    before = (owner[None, :] == owner[:, None]) & (freq_ids[None, :] < freq_ids[:, None])
    rank_in = jnp.sum(before.astype(jnp.int32), axis=1)
    slot_of = owner * FCAP + rank_in
    targets = jnp.arange(slot_count, dtype=jnp.int32)
    return (slot_of[None, :] == targets[:, None]).astype(jnp.float32)


def partial_gram(matrices):
    return jnp.einsum("kip,kjp->kij", matrices, matrices, precision=lax.Precision.HIGHEST)


def finish_pass(matrices, totals, rows_total):
    gram = totals / rows_total
    identity = jnp.eye(gram.shape[-1], dtype=jnp.float32)
    diagonal_sum = jnp.trace(gram, axis1=1, axis2=2)
    gram = gram + jnp.where(diagonal_sum == 0.0, 1.0, 0.0)[:, None, None] * identity
    factor = jnp.linalg.cholesky(gram)
    inverse = jax.scipy.linalg.solve_triangular(
        factor, jnp.broadcast_to(identity, gram.shape), lower=True
    )
    return jnp.einsum("kij,kjp->kip", inverse, matrices, precision=lax.Precision.HIGHEST)


def local(snapshots, block_starts, owner):
    table = dft_table()
    samples, points = snapshots.shape
    block_count = block_starts.shape[0]
    tm_count = lax.axis_size("tm")
    space_count = lax.axis_size("space")
    rows_total = 2.0 * points * space_count
    column_count = block_count * tm_count
    offset = lax.axis_index("tm") * samples
    segments = jnp.stack(
        [
            lax.dynamic_slice_in_dim(snapshots, block_starts[block] - offset, NFFT, 0)
            for block in range(block_count)
        ]
    )
    spectra = jnp.einsum("fct,btp->fbcp", table, segments, precision=lax.Precision.HIGHEST)
    selector = slot_selector(owner, tm_count * FCAP)
    outgoing = jnp.einsum("lf,fbcp->lbcp", selector, spectra, precision=lax.Precision.HIGHEST)
    outgoing = outgoing.reshape(tm_count, FCAP, block_count, 2, points)
    received = lax.all_to_all(outgoing, "tm", split_axis=0, concat_axis=2, tiled=True)
    count = received.shape[1]
    matrices = received[0].reshape(count, column_count, 2 * points)
    for turn in range(2):
        partial_sums = partial_gram(matrices)
        totals = jnp.stack([lax.psum(partial_sums[item], "space") for item in range(count)])
        matrices = finish_pass(matrices, totals, rows_total)
    return matrices.reshape(count, column_count, 2, points)


def solution(mesh):
    placed = (P("tm", "space"), P("tm"), P())
    return jax.shard_map(
        local, mesh=mesh, in_specs=placed, out_specs=P("tm", None, None, "space"), check_vma=False
    )
```

profile of v0, /device:TPU:8, one launch (start us, length us, event | category | flops | bytes accessed | tf_op | source)
XLA Modules:
  0.0 621.2 jit_solution(3651869889522997822)
XLA Ops:
  0.0 1.6 fusion.31
  6.7 0.9 convert_reduce_fusion
  7.6 0.7 multiply_add_fusion.2
  8.3 2.4 bitcast_dynamic-update-slice_fusion.7
  10.7 2.4 bitcast_dynamic-update-slice_fusion.6
  13.1 2.4 bitcast_dynamic-update-slice_fusion.5
  15.5 2.4 bitcast_dynamic-update-slice_fusion.4
  17.9 2.4 bitcast_dynamic-update-slice_fusion.3
  20.2 2.4 bitcast_dynamic-update-slice_fusion.2
  22.7 2.4 bitcast_dynamic-update-slice_fusion.1
  25.1 2.4 bitcast_dynamic-update-slice_fusion
  27.5 7.5 %fusion.2 = f32[9,8,2,1024]{3,0,2,1:T(8,128)S(1)} fusion(f32[8,256,1024]{2,1,0:T(8,128)} %bitcast_dynamic-update-slice_fusion, f32[9,1,256]{2,0,1:T(8,128)S(1)} %get-tuple-element.35, f32[9,1,256]{2,0,1:T(8,128)S(1)} %get-tuple-element.36), kind=kOutput, calls=%fused_computation.2 | convolution fusion | flops 452989440 | bytes 8996864 | tf_op jit(solution)/shard_map/fct,btp->fbcp/dot_general | solution.py:60
  35.0 0.9 fusion.23
  35.9 1.8 copy.31
  37.7 5.7 all-to-all-start
  43.5 15.6 %all-to-all-done = f32[4,5,8,2,1024]{4,2,3,1,0:T(8,128)S(1)} async-done(((f32[4,5,8,2,1024]{4,2,3,1,0:T(8,128)}), f32[4,5,8,2,1024]{4,2,3,1,0:T(8,128)S(1)}, u32[]{:S(2)}, u32[]{:S(2)}) %all-to-all-start) | async-done | bytes 1310752 | tf_op jit(solution)/shard_map/all_to_all | solution.py:64
  59.1 0.1 copy.32
  59.2 1.2 fusion.32
  60.5 252.4 %all-reduce.1 = (f32[1,32,32]{1,2,0:T(8,128)S(1)}, f32[1,32,32]{1,2,0:T(8,128)S(1)}, f32[1,32,32]{1,2,0:T(8,128)S(1)}, f32[1,32,32]{1,2,0:T(8,128)S(1)}, f32[1,32,32]{1,2,0:T(8,128)S(1)}) all-reduce(f32[1,32,32]{1,2,0:T(8,128)S(1)} %get-tuple-element.26, ...), channel_id=1, replica_groups=mesh['space'=64,'tm'=4] {'space'}, use_global_device_ids=true, to_apply=%region_1.2 | all-reduce | flops 5120 | bytes 40960 | tf_op jit(solution)/shard_map/psum | solution.py:69
  313.0 0.1 select_reduce_fusion.3
  313.3 14.7 %custom-call.8 = f32[5,32,32]{2,1,0:T(8,128)S(1)} custom-call(f32[5,32,32]{2,1,0:T(8,128)S(1)} %fusion.10), custom_call_target="Cholesky" | custom-call | tf_op jit(solution)/shard_map/jit(cholesky)/cholesky | solution.py:38
  328.2 12.3 %custom-call.9 = f32[5,1,32,32]{2,3,1,0:T(8,128)S(1)} custom-call(f32[5,1,32,32]{3,2,1,0:T(8,128)S(1)} %select_bitcast_fusion.1), custom_call_target="InvertDiagBlocksLowerTriangular" | custom-call | tf_op jit(solution)/shard_map/jit(_solve_triangular)/vmap()/triangular_solve | solution.py:39
  340.6 0.3 fusion.8
  340.9 1.2 fusion.33
  342.1 1.2 fusion.34
  343.4 246.4 %all-reduce = (f32[1,32,32]{1,2,0:T(8,128)S(1)}, f32[1,32,32]{1,2,0:T(8,128)S(1)}, f32[1,32,32]{1,2,0:T(8,128)S(1)}, f32[1,32,32]{1,2,0:T(8,128)S(1)}, f32[1,32,32]{1,2,0:T(8,128)S(1)}) all-reduce(f32[1,32,32]{1,2,0:T(8,128)S(1)} %get-tuple-element.21, ...), channel_id=1, replica_groups=mesh['space'=64,'tm'=4] {'space'}, use_global_device_ids=true, to_apply=%region_9.12 | all-reduce | flops 5120 | bytes 40960 | tf_op jit(solution)/shard_map/psum | solution.py:69
  589.8 0.1 select_reduce_fusion.2
  590.2 14.7 %custom-call.10 = f32[5,32,32]{2,1,0:T(8,128)S(1)} custom-call(f32[5,32,32]{2,1,0:T(8,128)S(1)} %fusion.7), custom_call_target="Cholesky" | custom-call | tf_op jit(solution)/shard_map/jit(cholesky)/cholesky | solution.py:38
  605.1 12.3 %custom-call.11 = f32[5,1,32,32]{2,3,1,0:T(8,128)S(1)} custom-call(f32[5,1,32,32]{3,2,1,0:T(8,128)S(1)} %select_bitcast_fusion), custom_call_target="InvertDiagBlocksLowerTriangular" | custom-call | tf_op jit(solution)/shard_map/jit(_solve_triangular)/vmap()/triangular_solve | solution.py:39
  617.4 0.3 fusion.5
  617.7 1.2 fusion.35
  619.0 2.2 reshape.155
  (33 shorter events, 1.2 us)
Async XLA Ops:
  37.7 21.4 %all-to-all-start = ((f32[4,5,8,2,1024]{4,2,3,1,0:T(8,128)}), f32[4,5,8,2,1024]{4,2,3,1,0:T(8,128)S(1)}, u32[]{:S(2)}, u32[]{:S(2)}) async-start(f32[4,5,8,2,1024]{4,2,3,1,0:T(8,128)} %bitcast.22), calls=%async_computation | async-start | bytes 2621440 | tf_op jit(solution)/shard_map/all_to_all | solution.py:64
where the time goes:
time: 622 us; the launch traced here: 621 us
  blocking collectives  499 us (80%)
  other arithmetic  56.8 us (9%)
  local copies, waits for them, and re-layouts  25.1 us (4%)
  waiting for transfers between devices  15.6 us (3%)
  matrix products  14 us (2%)
    psum x2, blocking collectives, local(): lax.psum(partial_sums[item], 'space')  499 us
    another operation x7, other arithmetic, finish_pass(): factor = jnp.linalg.cholesky(gram)  29.6 us
    another operation x5, other arithmetic, finish_pass(): jax.scipy.linalg.solve_triangular(factor, jnp.broadcast_to(identity, gram...  24.8 us
    unnamed x15, local copies, waits for them, and re-layouts  16.8 us
    all_to_all x1, waiting for transfers between devices, local(): lax.all_to_all(outgoing, 'tm', split_axis=0, concat_axis=2, tiled=True)  15.6 us
  transfers between devices with their start and end apart: 1, of which 1 were waited for; matrix products, arithmetic and copies ran while one was open for 0% of the time, Pallas kernels for 0%

commit v1 on v0

--- a/solution.py
+++ b/solution.py
@@ -66,7 +66,9 @@
     matrices = received[0].reshape(count, column_count, 2 * points)
     for turn in range(2):
         partial_sums = partial_gram(matrices)
-        totals = jnp.stack([lax.psum(partial_sums[item], "space") for item in range(count)])
+        totals = jnp.stack(
+            [jnp.sum(lax.all_gather(partial_sums[item], "space"), axis=0) for item in range(count)]
+        )
         matrices = finish_pass(matrices, totals, rows_total)
     return matrices.reshape(count, column_count, 2, points)
 

time: 622 us -> 628 us (level); the launches traced: 621 us -> 618 us
    psum x2 -> x0, blocking collectives: 499 us -> none  [local(): lax.psum(partial_sums[item], 'space')]
    all_gather x0 -> x10, blocking collectives: none -> 494 us  [local(): lax.all_gather(partial_sums[item], 'space')]
where the time goes in v1:
time: 628 us; the launch traced here: 618 us
  blocking collectives  494 us (79%)
  other arithmetic  57.8 us (9%)
  local copies, waits for them, and re-layouts  25.9 us (4%)
  waiting for transfers between devices  15.6 us (2%)
  matrix products  14.1 us (2%)
    all_gather x10, blocking collectives, local(): lax.all_gather(partial_sums[item], 'space')  494 us
    another operation x7, other arithmetic, finish_pass(): factor = jnp.linalg.cholesky(gram)  29.6 us
    another operation x5, other arithmetic, finish_pass(): jax.scipy.linalg.solve_triangular(factor, jnp.broadcast_to(identity, gram...  24.8 us
    unnamed x15, local copies, waits for them, and re-layouts  16.8 us
    all_to_all x1, waiting for transfers between devices, local(): lax.all_to_all(outgoing, 'tm', split_axis=0, concat_axis=2, tiled=True)  15.6 us
  transfers between devices with their start and end apart: 1, of which 1 were waited for; matrix products, arithmetic and copies ran while one was open for 0% of the time, Pallas kernels for 0%

profile of v1, /device:TPU:8, one launch (start us, length us, event | category | flops | bytes accessed | tf_op | source)
XLA Modules:
  0.0 618.0 jit_solution(1398409949245148966)
XLA Ops:
  0.0 1.6 fusion.31
  8.3 2.4 bitcast_dynamic-update-slice_fusion.7
  10.7 2.4 bitcast_dynamic-update-slice_fusion.6
  13.1 2.4 bitcast_dynamic-update-slice_fusion.5
  15.5 2.4 bitcast_dynamic-update-slice_fusion.4
  17.9 2.4 bitcast_dynamic-update-slice_fusion.3
  20.2 2.4 bitcast_dynamic-update-slice_fusion.2
  22.7 2.4 bitcast_dynamic-update-slice_fusion.1
  25.1 2.4 bitcast_dynamic-update-slice_fusion
  27.5 7.5 %fusion.2 = f32[9,8,2,1024]{3,0,2,1:T(8,128)S(1)} fusion(f32[8,256,1024]{2,1,0:T(8,128)} %bitcast_dynamic-update-slice_fusion, f32[9,1,256]{2,0,1:T(8,128)S(1)} %get-tuple-element.25, f32[9,1,256]{2,0,1:T(8,128)S(1)} %get-tuple-element.26), kind=kOutput, calls=%fused_computation.2 | convolution fusion | flops 452989440 | bytes 8996864 | tf_op jit(solution)/shard_map/fct,btp->fbcp/dot_general | solution.py:60
  35.9 1.8 copy.29
  37.7 5.7 all-to-all-start
  43.5 15.6 %all-to-all-done = f32[4,5,8,2,1024]{4,2,3,1,0:T(8,128)S(1)} async-done(((f32[4,5,8,2,1024]{4,2,3,1,0:T(8,128)}), f32[4,5,8,2,1024]{4,2,3,1,0:T(8,128)S(1)}, u32[]{:S(2)}, u32[]{:S(2)}) %all-to-all-start) | async-done | bytes 1310752 | tf_op jit(solution)/shard_map/all_to_all | solution.py:64
  59.2 1.3 fusion.32
  60.6 53.5 %all_gather.30 = f32[64,32,32]{2,1,0:T(8,128)S(1)} all-gather(f32[1,32,32]{2,1,0:T(8,128)S(1)} %get-tuple-element.16), channel_id=1, replica_groups=mesh['space'=64,'tm'=4] {'space'}, dimensions={0}, use_global_device_ids=true | all-gather | bytes 266240 | tf_op jit(solution)/shard_map/all_gather | solution.py:70
  114.3 49.8 %all_gather.31 = f32[64,32,32]{2,1,0:T(8,128)S(1)} all-gather(f32[1,32,32]{2,1,0:T(8,128)S(1)} %get-tuple-element.15), channel_id=1, replica_groups=mesh['space'=64,'tm'=4] {'space'}, dimensions={0}, use_global_device_ids=true | all-gather | bytes 266240 | tf_op jit(solution)/shard_map/all_gather | solution.py:70
  164.2 48.1 %all_gather.32 = f32[64,32,32]{2,1,0:T(8,128)S(1)} all-gather(f32[1,32,32]{2,1,0:T(8,128)S(1)} %get-tuple-element.14), channel_id=1, replica_groups=mesh['space'=64,'tm'=4] {'space'}, dimensions={0}, use_global_device_ids=true | all-gather | bytes 266240 | tf_op jit(solution)/shard_map/all_gather | solution.py:70
  212.6 49.3 %all_gather.33 = f32[64,32,32]{2,1,0:T(8,128)S(1)} all-gather(f32[1,32,32]{2,1,0:T(8,128)S(1)} %get-tuple-element.13), channel_id=1, replica_groups=mesh['space'=64,'tm'=4] {'space'}, dimensions={0}, use_global_device_ids=true | all-gather | bytes 266240 | tf_op jit(solution)/shard_map/all_gather | solution.py:70
  262.0 48.3 %all_gather.34 = f32[64,32,32]{2,1,0:T(8,128)S(1)} all-gather(f32[1,32,32]{2,1,0:T(8,128)S(1)} %get-tuple-element.12), channel_id=1, replica_groups=mesh['space'=64,'tm'=4] {'space'}, dimensions={0}, use_global_device_ids=true | all-gather | bytes 266240 | tf_op jit(solution)/shard_map/all_gather | solution.py:70
  311.0 14.7 %custom-call.8 = f32[5,32,32]{2,1,0:T(8,128)S(1)} custom-call(f32[5,32,32]{2,1,0:T(8,128)S(1)} %fusion.10), custom_call_target="Cholesky" | custom-call | tf_op jit(solution)/shard_map/jit(cholesky)/cholesky | solution.py:38
  325.9 12.3 %custom-call.9 = f32[5,1,32,32]{2,3,1,0:T(8,128)S(1)} custom-call(f32[5,1,32,32]{3,2,1,0:T(8,128)S(1)} %select_bitcast_fusion.1), custom_call_target="InvertDiagBlocksLowerTriangular" | custom-call | tf_op jit(solution)/shard_map/jit(_solve_triangular)/vmap()/triangular_solve | solution.py:39
  338.5 1.2 fusion.33
  339.8 1.3 fusion.34
  341.1 49.3 %all_gather.35 = f32[64,32,32]{2,1,0:T(8,128)S(1)} all-gather(f32[1,32,32]{2,1,0:T(8,128)S(1)} %get-tuple-element.11), channel_id=1, replica_groups=mesh['space'=64,'tm'=4] {'space'}, dimensions={0}, use_global_device_ids=true | all-gather | bytes 266240 | tf_op jit(solution)/shard_map/all_gather | solution.py:70
  390.6 48.2 %all_gather.36 = f32[64,32,32]{2,1,0:T(8,128)S(1)} all-gather(f32[1,32,32]{2,1,0:T(8,128)S(1)} %get-tuple-element.10), channel_id=1, replica_groups=mesh['space'=64,'tm'=4] {'space'}, dimensions={0}, use_global_device_ids=true | all-gather | bytes 266240 | tf_op jit(solution)/shard_map/all_gather | solution.py:70
  438.9 49.5 %all_gather.37 = f32[64,32,32]{2,1,0:T(8,128)S(1)} all-gather(f32[1,32,32]{2,1,0:T(8,128)S(1)} %get-tuple-element.9), channel_id=1, replica_groups=mesh['space'=64,'tm'=4] {'space'}, dimensions={0}, use_global_device_ids=true | all-gather | bytes 266240 | tf_op jit(solution)/shard_map/all_gather | solution.py:70
  488.6 48.2 %all_gather.38 = f32[64,32,32]{2,1,0:T(8,128)S(1)} all-gather(f32[1,32,32]{2,1,0:T(8,128)S(1)} %get-tuple-element.8), channel_id=1, replica_groups=mesh['space'=64,'tm'=4] {'space'}, dimensions={0}, use_global_device_ids=true | all-gather | bytes 266240 | tf_op jit(solution)/shard_map/all_gather | solution.py:70
  537.0 49.3 %all_gather.39 = f32[64,32,32]{2,1,0:T(8,128)S(1)} all-gather(f32[1,32,32]{2,1,0:T(8,128)S(1)} %get-tuple-element.6), channel_id=1, replica_groups=mesh['space'=64,'tm'=4] {'space'}, dimensions={0}, use_global_device_ids=true | all-gather | bytes 266240 | tf_op jit(solution)/shard_map/all_gather | solution.py:70
  586.8 14.7 %custom-call.10 = f32[5,32,32]{2,1,0:T(8,128)S(1)} custom-call(f32[5,32,32]{2,1,0:T(8,128)S(1)} %fusion.7), custom_call_target="Cholesky" | custom-call | tf_op jit(solution)/shard_map/jit(cholesky)/cholesky | solution.py:38
  601.7 12.3 %custom-call.11 = f32[5,1,32,32]{2,3,1,0:T(8,128)S(1)} custom-call(f32[5,1,32,32]{3,2,1,0:T(8,128)S(1)} %select_bitcast_fusion), custom_call_target="InvertDiagBlocksLowerTriangular" | custom-call | tf_op jit(solution)/shard_map/jit(_solve_triangular)/vmap()/triangular_solve | solution.py:39
  614.4 1.2 fusion.35
  615.6 2.2 reshape.155
  (61 shorter events, 6.5 us)
Async XLA Ops:
  37.7 21.4 %all-to-all-start = ((f32[4,5,8,2,1024]{4,2,3,1,0:T(8,128)}), f32[4,5,8,2,1024]{4,2,3,1,0:T(8,128)S(1)}, u32[]{:S(2)}, u32[]{:S(2)}) async-start(f32[4,5,8,2,1024]{4,2,3,1,0:T(8,128)} %bitcast.22), calls=%async_computation | async-start | bytes 2621440 | tf_op jit(solution)/shard_map/all_to_all | solution.py:64
